TPU v7x, 32 devices: a whole 2x2x4 slice. The times are simulated.
32 devices in a mesh: dp: 4 (over y, x), fsdp: 8 (over z, core).
Axes of the slice: x: 2, y: 2, z: 4, core: 2. Of those that a mesh axis runs over, the one named last changes fastest.
Arguments:
- token_ids: int32 [32, 128], P(('dp', 'fsdp')), may hold values from 0 to 8191
- target_ids: int32 [32, 128], P(('dp', 'fsdp')), may hold values from 0 to 8191
- domain_ids: int32 [32, 1], P(('dp', 'fsdp')), may hold values from 0 to 21
- in_embed: bfloat16 [8192, 128], P('fsdp'), may hold values from -6 to 6
- out_embed: bfloat16 [8192, 128], P('fsdp'), may hold values from -42.426407 to 42.426407
- ref_norm1: bfloat16 [128], P('fsdp'), may hold values from 0.5 to 1.5
- ref_gate: bfloat16 [512, 128], P('fsdp'), may hold values from -0.5 to 0.5
- ref_up: bfloat16 [512, 128], P('fsdp'), may hold values from -0.5 to 0.5
- ref_down: bfloat16 [512, 128], P('fsdp'), may hold values from -0.25 to 0.25
- ref_norm2: bfloat16 [128], P('fsdp'), may hold values from 0.5 to 1.5
- prx_norm1: bfloat16 [128], P('fsdp'), may hold values from 0.5 to 1.5
- prx_gate: bfloat16 [512, 128], P('fsdp'), may hold values from -0.5 to 0.5
- prx_up: bfloat16 [512, 128], P('fsdp'), may hold values from -0.5 to 0.5
- prx_down: bfloat16 [512, 128], P('fsdp'), may hold values from -0.25 to 0.25
- prx_norm2: bfloat16 [128], P('fsdp'), may hold values from 0.5 to 1.5
- alpha_prev: float32 [22], replicated, may hold values from 0.01 to 0.1
Outputs:
- alpha_new: float32 [22], replicated
- grad_gate: float32 [512, 128], P('fsdp')
- grad_up: float32 [512, 128], P('fsdp')
- grad_down: float32 [512, 128], P('fsdp')
Inputs may be any that keep to these rules, and one draw needn't show every extreme that they name: `domain_ids`: every one of the 22 domains is the domain of at least one row.
All inputs are finite; a program needn't handle non-finite values.
Results may differ from a plain program's by a relative error of at most 0.0075.
The roundings to bfloat16 on the way count: a program that leaves them out, or rounds other values in their place, can miss the bound.
Values may be sent and summed in bfloat16 or wider, within the bound.
No kernel may reach another device: no remote copies, remote signals or barrier semaphores. Data moves between devices by JAX's collectives and lax.ppermute only.
A program may use at most 64 MiB of HBM per device.

v0:
```python
import math
import jax
import jax.numpy as jnp
from jax import lax
from jax.sharding import PartitionSpec as P

EPSILON = 1e-05
SMOOTHING = 0.001


def combined_all(value, axis, join):
    pieces = jax.tree.map(lambda part: lax.all_gather(part, axis), value)
    head = jax.tree.map(lambda part: part[0], pieces)
    tail = jax.tree.map(lambda part: part[1:], pieces)
    running, _ = lax.scan(lambda running, piece: (join(running, piece), None), head, tail)
    return running


def rms_scale(values):
    return lax.rsqrt(jnp.mean(values * values, axis=1, keepdims=True) + EPSILON)


def contract_last(left_side, right_side):
    return lax.dot_general(
        left_side, right_side, (((1,), (1,)), ((), ())), preferred_element_type=jnp.float32
    )


def contract_first(left_side, right_side):
    return lax.dot_general(
        left_side, right_side, (((0,), (0,)), ((), ())), preferred_element_type=jnp.float32
    )


def feed_forward(embedded, normed, weights):
    gate_weight, up_weight, down_weight, norm_first, norm_second = weights
    first_in = (normed * norm_first.astype(jnp.float32)).astype(jnp.bfloat16)
    gate_act = contract_last(first_in, gate_weight)
    up_act = contract_last(first_in, up_weight)
    hidden = (gate_act * jax.nn.sigmoid(gate_act) * up_act).astype(jnp.bfloat16)
    stream = embedded + jnp.dot(hidden, down_weight, preferred_element_type=jnp.float32)
    second_scale = rms_scale(stream)
    unit_stream = stream * second_scale
    second_in = (unit_stream * norm_second.astype(jnp.float32)).astype(jnp.bfloat16)
    return (second_in, (first_in, gate_act, up_act, hidden, second_scale, unit_stream))


def gather_layer(gate_shard, up_shard, down_shard, norm_first, norm_second):
    return (
        lax.all_gather(gate_shard, "fsdp", axis=0, tiled=True),
        lax.all_gather(up_shard, "fsdp", axis=0, tiled=True),
        lax.all_gather(down_shard, "fsdp", axis=0, tiled=True),
        lax.all_gather(norm_first, "fsdp", axis=0, tiled=True),
        lax.all_gather(norm_second, "fsdp", axis=0, tiled=True),
    )


def shard_stats(second_in, table, local_target):
    row_total = second_in.shape[0]
    block_rows = math.gcd(row_total, 512)
    block_count = row_total // block_rows
    column_range = jnp.arange(table.shape[0], dtype=jnp.int32)

    def shard_one_block(block):
        inputs, targets = block
        logits = contract_last(inputs, table)
        top_logit = jnp.max(logits, axis=1)
        exp_total = jnp.sum(jnp.exp(logits - top_logit[:, None]), axis=1)
        picked = jnp.sum(jnp.where(targets[:, None] == column_range[None, :], logits, 0.0), axis=1)
        return (top_logit, exp_total, picked)

    results = lax.map(
        shard_one_block,
        (
            second_in.reshape(block_count, block_rows, -1),
            local_target.reshape(block_count, block_rows),
        ),
    )
    return tuple((item.reshape(row_total) for item in results))


def combine_stats(first, second):
    merged = []
    for offset in range(0, len(first), 3):
        top_first, total_first, pick_first = (first[offset], first[offset + 1], first[offset + 2])
        top_second, total_second, pick_second = (
            second[offset],
            second[offset + 1],
            second[offset + 2],
        )
        top_logit = jnp.maximum(top_first, top_second)
        exp_total = total_first * jnp.exp(top_first - top_logit) + total_second * jnp.exp(
            top_second - top_logit
        )
        merged = merged + [top_logit, exp_total, pick_first + pick_second]
    return tuple(merged)


def body(
    token_ids,
    target_ids,
    domain_ids,
    in_embed,
    out_embed,
    ref_norm1,
    ref_gate,
    ref_up,
    ref_down,
    ref_norm2,
    prx_norm1,
    prx_gate,
    prx_up,
    prx_down,
    prx_norm2,
    alpha_prev,
):
    domain_total = alpha_prev.shape[0]
    rows_here, seq_len = token_ids.shape
    per_device = rows_here * seq_len
    vocab_here = in_embed.shape[0]
    width = in_embed.shape[1]
    fsdp_size = lax.axis_size("fsdp")
    vocab_start = lax.axis_index("fsdp") * vocab_here
    all_tokens, all_targets, all_domains = (
        lax.all_gather(token_ids, "fsdp", axis=0, tiled=True),
        lax.all_gather(target_ids, "fsdp", axis=0, tiled=True),
        lax.all_gather(domain_ids, "fsdp", axis=0, tiled=True),
    )
    token_local = all_tokens.reshape(-1) - vocab_start
    target_local = all_targets.reshape(-1) - vocab_start
    domain_flat = jnp.repeat(all_domains[:, 0], seq_len)
    domain_range = jnp.arange(domain_total, dtype=jnp.int32)
    dom_hits = (domain_flat[:, None] == domain_range[None, :]).astype(jnp.float32)
    inside = ((token_local >= 0) & (token_local < vocab_here)).astype(jnp.float32)
    picked_rows = (
        jnp.take(in_embed, jnp.clip(token_local, 0, vocab_here - 1), axis=0).astype(jnp.float32)
        * inside[:, None]
    )
    ref_weights = gather_layer(ref_gate, ref_up, ref_down, ref_norm1, ref_norm2)
    prx_weights = gather_layer(prx_gate, prx_up, prx_down, prx_norm1, prx_norm2)
    embedded = lax.psum_scatter(
        picked_rows.astype(jnp.bfloat16), "fsdp", scatter_dimension=0, tiled=True
    ).astype(jnp.float32)
    normed = embedded * rms_scale(embedded)
    ref_own = feed_forward(embedded, normed, ref_weights)[0]
    prx_own, saved_state = feed_forward(embedded, normed, prx_weights)
    ref_group, prx_group = (
        lax.all_gather(ref_own, "fsdp", axis=0, tiled=True),
        lax.all_gather(prx_own, "fsdp", axis=0, tiled=True),
    )
    ref_top, ref_sum, ref_pick = shard_stats(ref_group, out_embed, target_local)
    prx_top, prx_sum, prx_pick = shard_stats(prx_group, out_embed, target_local)
    merged = combined_all(
        (ref_top, ref_sum, ref_pick, prx_top, prx_sum, prx_pick), "fsdp", combine_stats
    )
    ref_loss = merged[0] + jnp.log(merged[1]) - merged[2]
    prx_total = merged[3] + jnp.log(merged[4])
    excess = jnp.maximum(prx_total - merged[5] - ref_loss, 0.0)
    total_sums, domain_counts = lax.psum(
        (jnp.sum(dom_hits * excess[:, None], axis=0), jnp.sum(dom_hits, axis=0)), "dp"
    )
    softmax_mix = jax.nn.softmax(jnp.log(alpha_prev) + total_sums / domain_counts)
    alpha_new = (1.0 - SMOOTHING) * softmax_mix + SMOOTHING / domain_total
    device_total = per_device * lax.axis_size("dp") * fsdp_size
    token_ratio = math.sqrt(device_total) * alpha_new / domain_counts
    token_weight = jnp.sum(dom_hits * token_ratio[None, :], axis=1)
    column_range = jnp.arange(vocab_here, dtype=jnp.int32)
    block_rows = math.gcd(per_device * lax.axis_size("fsdp"), 512)
    block_count = per_device * lax.axis_size("fsdp") // block_rows
    inputs = prx_group.reshape(block_count, block_rows, -1)
    totals = prx_total.reshape(block_count, block_rows)
    weights = token_weight.reshape(block_count, block_rows)
    targets = target_local.reshape(block_count, block_rows)

    def head_one_block(block):
        block_in, block_total, block_weight, block_target = block
        logits = contract_last(block_in, out_embed)
        probs = jnp.exp(logits - block_total[:, None])
        hits = (block_target[:, None] == column_range[None, :]).astype(jnp.float32)
        d_logits = (block_weight[:, None] * (probs - hits)).astype(jnp.bfloat16)
        return jnp.dot(d_logits, out_embed, preferred_element_type=jnp.float32)

    d_second = lax.psum_scatter(
        lax.map(head_one_block, (inputs, totals, weights, targets)).reshape(
            per_device * lax.axis_size("fsdp"), -1
        ),
        "fsdp",
        scatter_dimension=0,
        tiled=True,
    )
    first_in, gate_act, up_act, hidden, second_scale, unit_stream = saved_state
    d_unit = d_second * prx_weights[4].astype(jnp.float32)
    d_branch = (
        second_scale
        * (d_unit - unit_stream * jnp.mean(d_unit * unit_stream, axis=1, keepdims=True))
    ).astype(jnp.bfloat16)
    d_hidden = contract_last(d_branch, prx_weights[2])
    sigmoid_gate = jax.nn.sigmoid(gate_act)
    d_gate = (d_hidden * up_act * sigmoid_gate * (1.0 + gate_act * (1.0 - sigmoid_gate))).astype(
        jnp.bfloat16
    )
    d_up = (d_hidden * gate_act * sigmoid_gate).astype(jnp.bfloat16)
    partial_grad = jnp.concatenate(
        [
            contract_first(d_gate, first_in),
            contract_first(d_up, first_in),
            contract_first(hidden, d_branch),
        ],
        axis=1,
    )
    rounded = lax.optimization_barrier(partial_grad.astype(jnp.bfloat16))
    local_grad = lax.psum_scatter(
        rounded.astype(jnp.float32).astype(jnp.bfloat16), "fsdp", scatter_dimension=0, tiled=True
    ).astype(jnp.float32)
    grad_shard = lax.psum(local_grad, "dp")
    return (
        alpha_new,
        grad_shard[:, :width],
        grad_shard[:, width : 2 * width],
        grad_shard[:, 2 * width :],
    )


def solution(mesh):
    placed = (
        P(("dp", "fsdp"), None),
        P(("dp", "fsdp"), None),
        P(("dp", "fsdp"), None),
        P("fsdp", None),
        P("fsdp", None),
        P("fsdp"),
        P("fsdp", None),
        P("fsdp", None),
        P("fsdp", None),
        P("fsdp"),
        P("fsdp"),
        P("fsdp", None),
        P("fsdp", None),
        P("fsdp", None),
        P("fsdp"),
        P(),
    )
    return jax.shard_map(
        body,
        mesh=mesh,
        in_specs=placed,
        out_specs=(P(), P("fsdp", None), P("fsdp", None), P("fsdp", None)),
        check_vma=False,
    )
```

profile of v0, /device:TPU:0, one launch (start us, length us, event | category | flops | bytes accessed | tf_op | source)
XLA Modules:
  0.0 369.3 jit_solution(6620996398305857346)
XLA Ops:
  7.4 13.7 %all-gather = s32[8,1,128]{2,1,0:T(1,128)S(1)} all-gather(s32[1,1,128]{2,1,0:T(1,128)} %bitcast.177), channel_id=1, replica_groups=mesh['dp'=4,'fsdp'=8] {'fsdp'}, dimensions={0}, use_global_device_ids=true | all-gather | bytes 4608 | tf_op jit(solution)/shard_map/all_gather | solution.py:125
  21.1 3.2 gather_fusion
  24.3 1.0 multiply_convert_fusion.1
  26.1 8.6 %all-gather.1 = s32[8,1,128]{2,1,0:T(1,128)S(1)} all-gather(s32[1,1,128]{2,1,0:T(1,128)S(1)} %bitcast.178), channel_id=1, replica_groups=mesh['dp'=4,'fsdp'=8] {'fsdp'}, dimensions={0}, use_global_device_ids=true | all-gather | bytes 4608 | tf_op jit(solution)/shard_map/all_gather | solution.py:126
  34.8 0.6 dynamic-slice
  35.4 0.7 bitcast_dynamic-update-slice_fusion
  36.1 14.0 %all_gather.78 = bf16[512,128]{1,0:T(8,128)(2,1)S(1)} all-gather(bf16[64,128]{1,0:T(8,128)(2,1)S(1)} %copy-done.2), channel_id=1, replica_groups=mesh['dp'=4,'fsdp'=8] {'fsdp'}, dimensions={0}, use_global_device_ids=true | all-gather | bytes 147456 | tf_op jit(solution)/shard_map/all_gather | solution.py:52
  50.1 7.2 %all-reduce = s32[8]{0:T(128)S(1)} all-reduce(s32[8]{0:T(128)S(1)} %bitcast_dynamic-update-slice_fusion), channel_id=1, replica_groups=mesh['dp'=4,'fsdp'=8] {'fsdp'}, use_global_device_ids=true, to_apply=%add | all-reduce | flops 8 | bytes 64
  59.0 13.9 %all-reduce.6 = (bf16[128]{0:T(256)(128)(2,1)S(1)}, bf16[128]{0:T(256)(128)(2,1)S(1)}, bf16[128]{0:T(256)(128)(2,1)S(1)}, bf16[128]{0:T(256)(128)(2,1)S(1)}) all-reduce(bf16[128]{0:T(256)(128)(2,1)S(1)} %dynamic-update-slice.1, bf16[128]{0:T(256)(128)(2,1)S(1)} %dynamic-update-slice.2, ...), channel_id=1, replica_groups=mesh['dp'=4,'fsdp'=8] {'fsdp'}, use_global_device_ids=true, to_apply=%add.1 | all-reduce | flops 512 | bytes 2048
  73.0 14.0 %all_gather.66 = bf16[512,128]{1,0:T(8,128)(2,1)S(1)} all-gather(bf16[64,128]{1,0:T(8,128)(2,1)S(1)} %copy-done.3), channel_id=1, replica_groups=mesh['dp'=4,'fsdp'=8] {'fsdp'}, dimensions={0}, use_global_device_ids=true | all-gather | bytes 147456 | tf_op jit(solution)/shard_map/all_gather | solution.py:50
  87.0 14.0 %all_gather.67 = bf16[512,128]{1,0:T(8,128)(2,1)S(1)} all-gather(bf16[64,128]{1,0:T(8,128)(2,1)S(1)} %copy-done.4), channel_id=1, replica_groups=mesh['dp'=4,'fsdp'=8] {'fsdp'}, dimensions={0}, use_global_device_ids=true | all-gather | bytes 147456 | tf_op jit(solution)/shard_map/all_gather | solution.py:51
  101.0 14.0 %all_gather.68 = bf16[512,128]{1,0:T(8,128)(2,1)S(1)} all-gather(bf16[64,128]{1,0:T(8,128)(2,1)S(1)} %copy-done.5), channel_id=1, replica_groups=mesh['dp'=4,'fsdp'=8] {'fsdp'}, dimensions={0}, use_global_device_ids=true | all-gather | bytes 147456 | tf_op jit(solution)/shard_map/all_gather | solution.py:52
  114.9 14.0 %all_gather.76 = bf16[512,128]{1,0:T(8,128)(2,1)S(1)} all-gather(bf16[64,128]{1,0:T(8,128)(2,1)S(1)} %copy-done.6), channel_id=1, replica_groups=mesh['dp'=4,'fsdp'=8] {'fsdp'}, dimensions={0}, use_global_device_ids=true | all-gather | bytes 147456 | tf_op jit(solution)/shard_map/all_gather | solution.py:50
  128.9 14.0 %all_gather.77 = bf16[512,128]{1,0:T(8,128)(2,1)S(1)} all-gather(bf16[64,128]{1,0:T(8,128)(2,1)S(1)} %copy-done.7), channel_id=1, replica_groups=mesh['dp'=4,'fsdp'=8] {'fsdp'}, dimensions={0}, use_global_device_ids=true | all-gather | bytes 147456 | tf_op jit(solution)/shard_map/all_gather | solution.py:51
  142.9 0.9 copy.53
  144.7 13.1 %all_gather.70 = bf16[1024,128]{0,1:T(8,128)(2,1)S(1)} all-gather(bf16[128,128]{0,1:T(8,128)(2,1)S(1)} %multiply_convert_fusion.9), channel_id=1, replica_groups=mesh['dp'=4,'fsdp'=8] {'fsdp'}, dimensions={0}, use_global_device_ids=true | all-gather | bytes 294912 | tf_op jit(solution)/shard_map/all_gather | solution.py:148
  158.0 3.0 while.62
  158.6 0.8 select_reduce_fusion.6
  160.1 0.8 select_reduce_fusion.6
  161.0 14.0 %all-gather.3 = f32[8,1,1024]{2,1,0:T(1,128)S(1)} all-gather(f32[1,1,1024]{2,1,0:T(1,128)S(1)} %reshape.171), channel_id=1, replica_groups=mesh['dp'=4,'fsdp'=8] {'fsdp'}, dimensions={0}, use_global_device_ids=true | all-gather | bytes 36864 | tf_op jit(solution)/shard_map/all_gather | solution.py:12
  175.1 14.0 %all-gather.2 = f32[8,1,1024]{2,1,0:T(1,128)S(1)} all-gather(f32[1,1,1024]{2,1,0:T(1,128)S(1)} %reshape.169), channel_id=1, replica_groups=mesh['dp'=4,'fsdp'=8] {'fsdp'}, dimensions={0}, use_global_device_ids=true | all-gather | bytes 36864 | tf_op jit(solution)/shard_map/all_gather | solution.py:12
  189.1 14.0 %all-gather.4 = f32[8,1,1024]{2,1,0:T(1,128)S(1)} all-gather(f32[1,1,1024]{2,1,0:T(1,128)S(1)} %reshape.173), channel_id=1, replica_groups=mesh['dp'=4,'fsdp'=8] {'fsdp'}, dimensions={0}, use_global_device_ids=true | all-gather | bytes 36864 | tf_op jit(solution)/shard_map/all_gather | solution.py:12
  204.0 13.3 %all_gather.80 = bf16[1024,128]{0,1:T(8,128)(2,1)S(1)} all-gather(bf16[128,128]{0,1:T(8,128)(2,1)S(1)} %multiply_convert_fusion.8), channel_id=1, replica_groups=mesh['dp'=4,'fsdp'=8] {'fsdp'}, dimensions={0}, use_global_device_ids=true | all-gather | bytes 294912 | tf_op jit(solution)/shard_map/all_gather | solution.py:149
  217.5 3.0 while.63
  218.1 0.8 select_reduce_fusion.7
  219.6 0.8 select_reduce_fusion.7
  220.5 14.0 %all-gather.6 = f32[8,1,1024]{2,1,0:T(1,128)S(1)} all-gather(f32[1,1,1024]{2,1,0:T(1,128)S(1)} %reshape.177), channel_id=1, replica_groups=mesh['dp'=4,'fsdp'=8] {'fsdp'}, dimensions={0}, use_global_device_ids=true | all-gather | bytes 36864 | tf_op jit(solution)/shard_map/all_gather | solution.py:12
  234.5 14.0 %all-gather.5 = f32[8,1,1024]{2,1,0:T(1,128)S(1)} all-gather(f32[1,1,1024]{2,1,0:T(1,128)S(1)} %reshape.175), channel_id=1, replica_groups=mesh['dp'=4,'fsdp'=8] {'fsdp'}, dimensions={0}, use_global_device_ids=true | all-gather | bytes 36864 | tf_op jit(solution)/shard_map/all_gather | solution.py:12
  248.6 14.0 %all-gather.7 = f32[8,1,1024]{2,1,0:T(1,128)S(1)} all-gather(f32[1,1,1024]{2,1,0:T(1,128)S(1)} %reshape.179), channel_id=1, replica_groups=mesh['dp'=4,'fsdp'=8] {'fsdp'}, dimensions={0}, use_global_device_ids=true | all-gather | bytes 36864 | tf_op jit(solution)/shard_map/all_gather | solution.py:12
  262.7 1.1 while.61
  263.9 9.9 %all-reduce.5 = (f32[22]{0:T(128)S(1)}, f32[22]{0:T(128)S(1)}) all-reduce(f32[22]{0:T(128)S(1)} %get-tuple-element.346, f32[22]{0:T(128)S(1)} %get-tuple-element.347), channel_id=1, replica_groups=mesh['dp'=4,'fsdp'=8] {'dp'}, use_global_device_ids=true, to_apply=%region_19.20 | all-reduce | flops 44 | bytes 352 | tf_op jit(solution)/shard_map/psum | solution.py:159
  273.9 0.6 fusion.60
  274.5 1.2 fusion.53
  275.7 1.8 multiply_divide_fusion
  277.7 1.8 while.64
  277.7 0.8 fusion.97
  278.6 0.8 fusion.97
  279.5 1.0 copy.51
  280.5 27.4 %reduce-scatter.8.cloned.1.call-done = f32[128,128]{0,1:T(8,128)} async-done(((f32[1024,128]{0,1:T(8,128)}), f32[128,128]{0,1:T(8,128)}) %reduce-scatter.8.cloned.1.call-update) | async-done | bytes 65552 | tf_op jit(solution)/shard_map/reduce_scatter | solution.py:183
  307.9 0.9 multiply_reduce_fusion
  308.9 0.9 multiply_convert_fusion.7
  310.7 0.9 copy.54
  311.7 29.0 %reduce-scatter.12.cloned.1.call-done = bf16[64,384]{1,0:T(8,128)(2,1)} async-done(((bf16[512,384]{1,0:T(8,128)(2,1)}), bf16[64,384]{1,0:T(8,128)(2,1)}) %reduce-scatter.12.cloned.1.call-update) | async-done | bytes 49168
  340.7 0.9 copy.55
  341.6 19.0 %all-reduce.8 = f32[64,384]{0,1:T(8,128)S(1)} all-reduce(bf16[64,384]{0,1:T(8,128)(2,1)S(1)} %copy.55), channel_id=1, replica_groups=mesh['dp'=4,'fsdp'=8] {'dp'}, use_global_device_ids=true, to_apply=%region_28.29 | all-reduce | flops 24576 | bytes 147456 | tf_op jit(solution)/shard_map/psum | solution.py:215
  360.7 0.7 copy.49
  361.4 0.7 copy.48
  362.1 0.7 copy.47
  (193 shorter events, 8.1 us)
Async XLA Ops:
  7.2 13.9 %copy-start = (bf16[1024,128]{1,0:T(8,128)(2,1)S(1)}, bf16[1024,128]{1,0:T(8,128)(2,1)}, u32[]{:S(2)}) copy-start(bf16[1024,128]{1,0:T(8,128)(2,1)} %param.27) | copy-start | bytes 786436
  7.2 27.6 %copy-start.14 = (u32[32]{0:T(128)S(1)}, u32[32]{0:T(128)}, u32[]{:S(2)}) copy-start(u32[32]{0:T(128)} %constant.110) | copy-start | bytes 388
  7.2 18.9 %copy-start.8 = (s32[1,128]{1,0:T(1,128)S(1)}, s32[1,128]{1,0:T(1,128)}, u32[]{:S(2)}) copy-start(s32[1,128]{1,0:T(1,128)} %param.25) | copy-start | bytes 1540
  7.2 28.9 %copy-start.2 = (bf16[64,128]{1,0:T(8,128)(2,1)S(1)}, bf16[64,128]{1,0:T(8,128)(2,1)}, u32[]{:S(2)}) copy-start(bf16[64,128]{1,0:T(8,128)(2,1)} %param.37) | copy-start | bytes 49156
  7.2 50.8 %copy-start.10 = (bf16[16]{0:T(256)(128)(2,1)S(1)}, bf16[16]{0:T(256)(128)(2,1)}, u32[]{:S(2)}) copy-start(bf16[16]{0:T(256)(128)(2,1)} %param.34) | copy-start | bytes 100
  7.2 51.1 %copy-start.11 = (bf16[16]{0:T(256)(128)(2,1)S(1)}, bf16[16]{0:T(256)(128)(2,1)}, u32[]{:S(2)}) copy-start(bf16[16]{0:T(256)(128)(2,1)} %param.33) | copy-start | bytes 100
  7.2 51.3 %copy-start.12 = (bf16[16]{0:T(256)(128)(2,1)S(1)}, bf16[16]{0:T(256)(128)(2,1)}, u32[]{:S(2)}) copy-start(bf16[16]{0:T(256)(128)(2,1)} %param.29) | copy-start | bytes 100
  7.2 51.5 %copy-start.13 = (bf16[16]{0:T(256)(128)(2,1)S(1)}, bf16[16]{0:T(256)(128)(2,1)}, u32[]{:S(2)}) copy-start(bf16[16]{0:T(256)(128)(2,1)} %param.38) | copy-start | bytes 100
  7.3 65.8 %copy-start.3 = (bf16[64,128]{1,0:T(8,128)(2,1)S(1)}, bf16[64,128]{1,0:T(8,128)(2,1)}, u32[]{:S(2)}) copy-start(bf16[64,128]{1,0:T(8,128)(2,1)} %param.30) | copy-start | bytes 49156
  7.3 79.7 %copy-start.4 = (bf16[64,128]{1,0:T(8,128)(2,1)S(1)}, bf16[64,128]{1,0:T(8,128)(2,1)}, u32[]{:S(2)}) copy-start(bf16[64,128]{1,0:T(8,128)(2,1)} %param.31) | copy-start | bytes 49156
  7.3 93.7 %copy-start.5 = (bf16[64,128]{1,0:T(8,128)(2,1)S(1)}, bf16[64,128]{1,0:T(8,128)(2,1)}, u32[]{:S(2)}) copy-start(bf16[64,128]{1,0:T(8,128)(2,1)} %param.32) | copy-start | bytes 49156
  7.3 107.6 %copy-start.6 = (bf16[64,128]{1,0:T(8,128)(2,1)S(1)}, bf16[64,128]{1,0:T(8,128)(2,1)}, u32[]{:S(2)}) copy-start(bf16[64,128]{1,0:T(8,128)(2,1)} %param.35) | copy-start | bytes 49156
  7.3 121.6 %copy-start.7 = (bf16[64,128]{1,0:T(8,128)(2,1)S(1)}, bf16[64,128]{1,0:T(8,128)(2,1)}, u32[]{:S(2)}) copy-start(bf16[64,128]{1,0:T(8,128)(2,1)} %param.36) | copy-start | bytes 49156
  7.3 135.6 %reduce-scatter.10.cloned.1.call-start = ((), (), s32[]{:S(2)}) async-start(), calls=%async_computation.4 | async-start | bytes 294912
  25.4 132.7 %copy-start.1 = (bf16[1024,128]{1,0:T(8,128)(2,1)S(1)}, bf16[1024,128]{1,0:T(8,128)(2,1)}, u32[]{:S(2)}) copy-start(bf16[1024,128]{1,0:T(8,128)(2,1)} %param.28) | copy-start | bytes 786436
  25.4 282.5 %reduce-scatter.8.cloned.1.call-start = ((), (), s32[]{:S(2)}) async-start(), calls=%async_computation.3 | async-start | bytes 589824 | tf_op jit(solution)/shard_map/reduce_scatter | solution.py:183
  217.5 56.4 %copy-start.9 = (f32[22]{0:T(128)S(1)}, f32[22]{0:T(128)}, u32[]{:S(2)}) copy-start(f32[22]{0:T(128)} %param.39) | copy-start | bytes 268
  280.5 60.2 %reduce-scatter.12.cloned.1.call-start = ((), (), s32[]{:S(2)}) async-start(), calls=%async_computation.5 | async-start | bytes 442368
Sparse Core Ops, SparseCore 0:
  25.5 28.6 reduce-scatter.9
  280.6 27.2 reduce-scatter.7
  311.8 28.8 reduce-scatter.11
where the time goes:
time: 370 us; the launch traced here: 369 us
  blocking collectives  267 us (72%)
  waiting for transfers between devices  56.4 us (15%)
  between operations  15.6 us (4%)
  local copies, waits for them, and re-layouts  12.9 us (3%)
  other arithmetic  10.5 us (3%)
  matrix products  6.23 us (2%)
    all_gather x6, blocking collectives, combined_all(): pieces = jax.tree.map(lambda part: lax.all_gather(part, axis), value)  84 us
    unnamed x5, waiting for transfers between devices  29.1 us
    all_gather x2, blocking collectives, gather_layer(): lax.all_gather(down_shard, 'fsdp', axis=0, tiled=True)  28 us
    all_gather x2, blocking collectives, gather_layer(): lax.all_gather(gate_shard, 'fsdp', axis=0, tiled=True)  27.9 us
    all_gather x2, blocking collectives, gather_layer(): lax.all_gather(up_shard, 'fsdp', axis=0, tiled=True)  27.9 us
    reduce_scatter x1, waiting for transfers between devices, body(): lax.psum_scatter(lax.map(head_one_block, (inputs, totals, weights, target...  27.4 us
    unnamed x2, blocking collectives  21.2 us
    psum x1, blocking collectives, body(): grad_shard = lax.psum(local_grad, 'dp')  19 us
  transfers between devices with their start and end apart: 3, of which 2 were waited for; matrix products, arithmetic and copies ran while one was open for 1% of the time, Pallas kernels for 0%

commit v1 on v0

--- a/solution.py
+++ b/solution.py
@@ -212,7 +212,8 @@
     local_grad = lax.psum_scatter(
         rounded.astype(jnp.float32).astype(jnp.bfloat16), "fsdp", scatter_dimension=0, tiled=True
     ).astype(jnp.float32)
-    grad_shard = lax.psum(local_grad, "dp")
+    parts = lax.all_gather(local_grad, "dp")
+    grad_shard = jnp.sum(parts, axis=0)
     return (
         alpha_new,
         grad_shard[:, :width],

time: 370 us -> 369 us (level)
  blocking collectives: 267 us -> 258 us
    reduce_scatter x0 -> x1, waiting for transfers between devices: none -> 29.1 us  [body(): lax.psum_scatter(rounded.astype(jnp.float32).astype(jnp.bfloat16), 'fsdp'...]
    unnamed x5 -> x4, waiting for transfers between devices: 29.1 us -> 0.05 us
    psum x1 -> x0, blocking collectives: 19 us -> none  [body(): grad_shard = lax.psum(local_grad, 'dp')]
    all_gather x0 -> x1, blocking collectives: none -> 9.47 us  [body(): parts = lax.all_gather(local_grad, 'dp')]
    unnamed x61 -> x71, local copies, waits for them, and re-layouts: 7.57 us -> 6.84 us
where the time goes in v1:
time: 369 us; the launch traced here: 368 us
  blocking collectives  258 us (70%)
  waiting for transfers between devices  56.5 us (15%)
  local copies, waits for them, and re-layouts  15.7 us (4%)
  between operations  15.7 us (4%)
  other arithmetic  12 us (3%)
  matrix products  9.23 us (3%)
    all_gather x6, blocking collectives, combined_all(): pieces = jax.tree.map(lambda part: lax.all_gather(part, axis), value)  84 us
    reduce_scatter x1, waiting for transfers between devices, body(): lax.psum_scatter(rounded.astype(jnp.float32).astype(jnp.bfloat16), 'fsdp'...  29.1 us
    all_gather x2, blocking collectives, gather_layer(): lax.all_gather(up_shard, 'fsdp', axis=0, tiled=True)  29 us
    all_gather x2, blocking collectives, gather_layer(): lax.all_gather(down_shard, 'fsdp', axis=0, tiled=True)  28 us
    all_gather x2, blocking collectives, gather_layer(): lax.all_gather(gate_shard, 'fsdp', axis=0, tiled=True)  27.9 us
    reduce_scatter x1, waiting for transfers between devices, body(): lax.psum_scatter(lax.map(head_one_block, (inputs, totals, weights, target...  27.4 us
    unnamed x2, blocking collectives  21.2 us
    all_gather x1, blocking collectives, body(): lax.all_gather(token_ids, 'fsdp', axis=0, tiled=True)  13.7 us
  transfers between devices with their start and end apart: 3, of which 2 were waited for; matrix products, arithmetic and copies ran while one was open for 1% of the time, Pallas kernels for 0%

profile of v1, /device:TPU:0, one launch (start us, length us, event | category | flops | bytes accessed | tf_op | source)
XLA Modules:
  0.0 368.1 jit_solution(3586796388426275132)
XLA Ops:
  7.4 13.7 %all-gather.1 = s32[8,1,128]{2,1,0:T(1,128)S(1)} all-gather(s32[1,1,128]{2,1,0:T(1,128)} %bitcast.179), channel_id=1, replica_groups=mesh['dp'=4,'fsdp'=8] {'fsdp'}, dimensions={0}, use_global_device_ids=true | all-gather | bytes 4608 | tf_op jit(solution)/shard_map/all_gather | solution.py:125
  21.1 3.2 gather_fusion
  24.3 1.0 multiply_convert_fusion.1
  26.1 8.6 %all-gather.2 = s32[8,1,128]{2,1,0:T(1,128)S(1)} all-gather(s32[1,1,128]{2,1,0:T(1,128)S(1)} %bitcast.180), channel_id=1, replica_groups=mesh['dp'=4,'fsdp'=8] {'fsdp'}, dimensions={0}, use_global_device_ids=true | all-gather | bytes 4608 | tf_op jit(solution)/shard_map/all_gather | solution.py:126
  35.4 0.7 bitcast_dynamic-update-slice_fusion
  36.1 14.0 %all_gather.77 = bf16[512,128]{1,0:T(8,128)(2,1)S(1)} all-gather(bf16[64,128]{1,0:T(8,128)(2,1)S(1)} %copy-done.3), channel_id=1, replica_groups=mesh['dp'=4,'fsdp'=8] {'fsdp'}, dimensions={0}, use_global_device_ids=true | all-gather | bytes 147456 | tf_op jit(solution)/shard_map/all_gather | solution.py:52
  50.1 7.2 %all-reduce = s32[8]{0:T(128)S(1)} all-reduce(s32[8]{0:T(128)S(1)} %bitcast_dynamic-update-slice_fusion), channel_id=1, replica_groups=mesh['dp'=4,'fsdp'=8] {'fsdp'}, use_global_device_ids=true, to_apply=%add | all-reduce | flops 8 | bytes 64
  59.0 13.9 %all-reduce.6 = (bf16[128]{0:T(256)(128)(2,1)S(1)}, bf16[128]{0:T(256)(128)(2,1)S(1)}, bf16[128]{0:T(256)(128)(2,1)S(1)}, bf16[128]{0:T(256)(128)(2,1)S(1)}) all-reduce(bf16[128]{0:T(256)(128)(2,1)S(1)} %dynamic-update-slice.1, bf16[128]{0:T(256)(128)(2,1)S(1)} %dynamic-update-slice.2, ...), channel_id=1, replica_groups=mesh['dp'=4,'fsdp'=8] {'fsdp'}, use_global_device_ids=true, to_apply=%add.1 | all-reduce | flops 512 | bytes 2048
  73.0 14.0 %all_gather.76 = bf16[512,128]{1,0:T(8,128)(2,1)S(1)} all-gather(bf16[64,128]{1,0:T(8,128)(2,1)S(1)} %copy-done.4), channel_id=1, replica_groups=mesh['dp'=4,'fsdp'=8] {'fsdp'}, dimensions={0}, use_global_device_ids=true | all-gather | bytes 147456 | tf_op jit(solution)/shard_map/all_gather | solution.py:51
  87.0 14.0 %all_gather.75 = bf16[512,128]{1,0:T(8,128)(2,1)S(1)} all-gather(bf16[64,128]{1,0:T(8,128)(2,1)S(1)} %copy-done.5), channel_id=1, replica_groups=mesh['dp'=4,'fsdp'=8] {'fsdp'}, dimensions={0}, use_global_device_ids=true | all-gather | bytes 147456 | tf_op jit(solution)/shard_map/all_gather | solution.py:50
  101.0 14.0 %all_gather.85 = bf16[512,128]{1,0:T(8,128)(2,1)S(1)} all-gather(bf16[64,128]{1,0:T(8,128)(2,1)S(1)} %copy-done.6), channel_id=1, replica_groups=mesh['dp'=4,'fsdp'=8] {'fsdp'}, dimensions={0}, use_global_device_ids=true | all-gather | bytes 147456 | tf_op jit(solution)/shard_map/all_gather | solution.py:50
  115.0 15.0 %all_gather.86 = bf16[512,128]{1,0:T(8,128)(2,1)} all-gather(bf16[64,128]{1,0:T(8,128)(2,1)S(1)} %copy-done.7), channel_id=1, replica_groups=mesh['dp'=4,'fsdp'=8] {'fsdp'}, dimensions={0}, use_global_device_ids=true | all-gather | bytes 147456 | tf_op jit(solution)/shard_map/all_gather | solution.py:51
  130.0 14.0 %all_gather.87 = bf16[512,128]{1,0:T(8,128)(2,1)S(1)} all-gather(bf16[64,128]{1,0:T(8,128)(2,1)S(1)} %copy-done.8), channel_id=1, replica_groups=mesh['dp'=4,'fsdp'=8] {'fsdp'}, dimensions={0}, use_global_device_ids=true | all-gather | bytes 147456 | tf_op jit(solution)/shard_map/all_gather | solution.py:52
  144.0 0.9 copy.64
  145.8 13.1 %all_gather.79 = bf16[1024,128]{0,1:T(8,128)(2,1)S(1)} all-gather(bf16[128,128]{0,1:T(8,128)(2,1)S(1)} %multiply_convert_fusion.9), channel_id=1, replica_groups=mesh['dp'=4,'fsdp'=8] {'fsdp'}, dimensions={0}, use_global_device_ids=true | all-gather | bytes 294912 | tf_op jit(solution)/shard_map/all_gather | solution.py:148
  159.1 2.9 while.62
  159.7 0.8 select_reduce_fusion.6
  161.2 0.8 select_reduce_fusion.6
  162.1 14.0 %all-gather.3 = f32[8,1,1024]{2,1,0:T(1,128)S(1)} all-gather(f32[1,1,1024]{2,1,0:T(1,128)S(1)} %reshape.171), channel_id=1, replica_groups=mesh['dp'=4,'fsdp'=8] {'fsdp'}, dimensions={0}, use_global_device_ids=true | all-gather | bytes 36864 | tf_op jit(solution)/shard_map/all_gather | solution.py:12
  176.7 14.0 %all-gather.4 = f32[8,1,1024]{2,1,0:T(1,128)S(1)} all-gather(f32[1,1,1024]{2,1,0:T(1,128)S(1)} %reshape.173), channel_id=1, replica_groups=mesh['dp'=4,'fsdp'=8] {'fsdp'}, dimensions={0}, use_global_device_ids=true | all-gather | bytes 36864 | tf_op jit(solution)/shard_map/all_gather | solution.py:12
  191.4 14.0 %all-gather.5 = f32[8,1,1024]{2,1,0:T(1,128)S(1)} all-gather(f32[1,1,1024]{2,1,0:T(1,128)S(1)} %reshape.175), channel_id=1, replica_groups=mesh['dp'=4,'fsdp'=8] {'fsdp'}, dimensions={0}, use_global_device_ids=true | all-gather | bytes 36864 | tf_op jit(solution)/shard_map/all_gather | solution.py:12
  206.3 1.9 multiply_convert_fusion.4
  208.6 13.3 %all_gather.89 = bf16[1024,128]{0,1:T(8,128)(2,1)S(1)} all-gather(bf16[128,128]{0,1:T(8,128)(2,1)S(1)} %multiply_convert_fusion.8), channel_id=1, replica_groups=mesh['dp'=4,'fsdp'=8] {'fsdp'}, dimensions={0}, use_global_device_ids=true | all-gather | bytes 294912 | tf_op jit(solution)/shard_map/all_gather | solution.py:149
  222.1 2.9 while.63
  222.7 0.8 select_reduce_fusion.7
  224.1 0.8 select_reduce_fusion.7
  225.0 14.0 %all-gather.6 = f32[8,1,1024]{2,1,0:T(1,128)S(1)} all-gather(f32[1,1,1024]{2,1,0:T(1,128)S(1)} %reshape.177), channel_id=1, replica_groups=mesh['dp'=4,'fsdp'=8] {'fsdp'}, dimensions={0}, use_global_device_ids=true | all-gather | bytes 36864 | tf_op jit(solution)/shard_map/all_gather | solution.py:12
  239.1 14.0 %all-gather.7 = f32[8,1,1024]{2,1,0:T(1,128)S(1)} all-gather(f32[1,1,1024]{2,1,0:T(1,128)S(1)} %reshape.179), channel_id=1, replica_groups=mesh['dp'=4,'fsdp'=8] {'fsdp'}, dimensions={0}, use_global_device_ids=true | all-gather | bytes 36864 | tf_op jit(solution)/shard_map/all_gather | solution.py:12
  253.1 14.0 %all-gather.8 = f32[8,1,1024]{2,1,0:T(1,128)S(1)} all-gather(f32[1,1,1024]{2,1,0:T(1,128)S(1)} %reshape.181), channel_id=1, replica_groups=mesh['dp'=4,'fsdp'=8] {'fsdp'}, dimensions={0}, use_global_device_ids=true | all-gather | bytes 36864 | tf_op jit(solution)/shard_map/all_gather | solution.py:12
  267.1 0.8 copy.85
  267.9 0.8 copy.84
  268.6 0.8 copy.83
  269.4 1.1 while.61
  270.7 9.9 %all-reduce.5 = (f32[22]{0:T(128)S(1)}, f32[22]{0:T(128)S(1)}) all-reduce(f32[22]{0:T(128)S(1)} %get-tuple-element.377, f32[22]{0:T(128)S(1)} %get-tuple-element.376), channel_id=1, replica_groups=mesh['dp'=4,'fsdp'=8] {'dp'}, use_global_device_ids=true, to_apply=%region_17.18 | all-reduce | flops 44 | bytes 352 | tf_op jit(solution)/shard_map/psum | solution.py:159
  280.6 1.3 fusion.60
  281.9 1.2 fusion.53
  283.2 1.8 multiply_divide_fusion
  285.1 3.2 while.64
  285.1 1.5 fusion.97
  286.7 1.6 fusion.97
  288.3 2.1 copy.62
  290.4 27.4 %reduce-scatter.8.cloned.1.call-done = f32[128,128]{0,1:T(8,128)} async-done(((f32[1024,128]{0,1:T(8,128)}), f32[128,128]{0,1:T(8,128)}) %reduce-scatter.8.cloned.1.call-update) | async-done | bytes 65552 | tf_op jit(solution)/shard_map/reduce_scatter | solution.py:183
  317.8 0.9 multiply_reduce_fusion
  318.7 0.9 multiply_convert_fusion.7
  320.7 0.9 copy.65
  321.6 29.1 %reduce-scatter.12.cloned.1.call-done = bf16[64,384]{1,0:T(8,128)(2,1)} async-done(((bf16[512,384]{1,0:T(8,128)(2,1)}), bf16[64,384]{1,0:T(8,128)(2,1)}) %reduce-scatter.12.cloned.1.call-update) | async-done | bytes 49168 | tf_op jit(solution)/shard_map/reduce_scatter | solution.py:212
  350.6 0.8 all_gather.96
  351.4 9.5 %all-gather = f32[256,384]{1,0:T(8,128)S(1)} all-gather(f32[64,384]{1,0:T(8,128)S(1)} %all_gather.96), channel_id=2, replica_groups=mesh['dp'=4,'fsdp'=8] {'dp'}, dimensions={0}, use_global_device_ids=true | all-gather | bytes 491520 | tf_op jit(solution)/shard_map/all_gather | solution.py:215
  (206 shorter events, 10.9 us)
Async XLA Ops:
  7.2 13.9 %copy-start = (bf16[1024,128]{1,0:T(8,128)(2,1)S(1)}, bf16[1024,128]{1,0:T(8,128)(2,1)}, u32[]{:S(2)}) copy-start(bf16[1024,128]{1,0:T(8,128)(2,1)} %param.27) | copy-start | bytes 786436
  7.2 27.6 %copy-start.20 = (u32[32]{0:T(128)S(1)}, u32[32]{0:T(128)}, u32[]{:S(2)}) copy-start(u32[32]{0:T(128)} %constant.110) | copy-start | bytes 388
  7.2 18.9 %copy-start.15 = (s32[1,128]{1,0:T(1,128)S(1)}, s32[1,128]{1,0:T(1,128)}, u32[]{:S(2)}) copy-start(s32[1,128]{1,0:T(1,128)} %param.25) | copy-start | bytes 1540
  7.2 28.9 %copy-start.3 = (bf16[64,128]{1,0:T(8,128)(2,1)S(1)}, bf16[64,128]{1,0:T(8,128)(2,1)}, u32[]{:S(2)}) copy-start(bf16[64,128]{1,0:T(8,128)(2,1)} %param.32) | copy-start | bytes 49156
  7.2 50.8 %copy-start.16 = (bf16[16]{0:T(256)(128)(2,1)S(1)}, bf16[16]{0:T(256)(128)(2,1)}, u32[]{:S(2)}) copy-start(bf16[16]{0:T(256)(128)(2,1)} %param.29) | copy-start | bytes 100
  7.2 51.1 %copy-start.17 = (bf16[16]{0:T(256)(128)(2,1)S(1)}, bf16[16]{0:T(256)(128)(2,1)}, u32[]{:S(2)}) copy-start(bf16[16]{0:T(256)(128)(2,1)} %param.33) | copy-start | bytes 100
  7.2 51.3 %copy-start.18 = (bf16[16]{0:T(256)(128)(2,1)S(1)}, bf16[16]{0:T(256)(128)(2,1)}, u32[]{:S(2)}) copy-start(bf16[16]{0:T(256)(128)(2,1)} %param.34) | copy-start | bytes 100
  7.2 51.5 %copy-start.19 = (bf16[16]{0:T(256)(128)(2,1)S(1)}, bf16[16]{0:T(256)(128)(2,1)}, u32[]{:S(2)}) copy-start(bf16[16]{0:T(256)(128)(2,1)} %param.38) | copy-start | bytes 100
  7.3 65.8 %copy-start.4 = (bf16[64,128]{1,0:T(8,128)(2,1)S(1)}, bf16[64,128]{1,0:T(8,128)(2,1)}, u32[]{:S(2)}) copy-start(bf16[64,128]{1,0:T(8,128)(2,1)} %param.31) | copy-start | bytes 49156
  7.3 79.7 %copy-start.5 = (bf16[64,128]{1,0:T(8,128)(2,1)S(1)}, bf16[64,128]{1,0:T(8,128)(2,1)}, u32[]{:S(2)}) copy-start(bf16[64,128]{1,0:T(8,128)(2,1)} %param.30) | copy-start | bytes 49156
  7.3 93.7 %copy-start.6 = (bf16[64,128]{1,0:T(8,128)(2,1)S(1)}, bf16[64,128]{1,0:T(8,128)(2,1)}, u32[]{:S(2)}) copy-start(bf16[64,128]{1,0:T(8,128)(2,1)} %param.35) | copy-start | bytes 49156
  7.3 107.7 %copy-start.7 = (bf16[64,128]{1,0:T(8,128)(2,1)S(1)}, bf16[64,128]{1,0:T(8,128)(2,1)}, u32[]{:S(2)}) copy-start(bf16[64,128]{1,0:T(8,128)(2,1)} %param.36) | copy-start | bytes 49156
  7.3 122.7 %copy-start.8 = (bf16[64,128]{1,0:T(8,128)(2,1)S(1)}, bf16[64,128]{1,0:T(8,128)(2,1)}, u32[]{:S(2)}) copy-start(bf16[64,128]{1,0:T(8,128)(2,1)} %param.37) | copy-start | bytes 49156
  7.3 136.7 %reduce-scatter.10.cloned.1.call-start = ((), (), s32[]{:S(2)}) async-start(), calls=%async_computation.4 | async-start | bytes 294912
  25.4 133.8 %copy-start.1 = (bf16[1024,128]{1,0:T(8,128)(2,1)S(1)}, bf16[1024,128]{1,0:T(8,128)(2,1)}, u32[]{:S(2)}) copy-start(bf16[1024,128]{1,0:T(8,128)(2,1)} %param.28) | copy-start | bytes 786436
  25.4 292.4 %reduce-scatter.8.cloned.1.call-start = ((), (), s32[]{:S(2)}) async-start(), calls=%async_computation.3 | async-start | bytes 589824 | tf_op jit(solution)/shard_map/reduce_scatter | solution.py:183
  73.0 133.3 %copy-start.13 = (f32[128]{0:T(128)}, f32[128]{0:T(128)S(1)}, u32[]{:S(2)}) copy-start(f32[128]{0:T(128)S(1)} %convert_element_type.82) | copy-start | bytes 1540
  145.0 61.3 %copy-start.11 = (f32[128]{0:T(128)}, f32[128]{0:T(128)S(1)}, u32[]{:S(2)}) copy-start(f32[128]{0:T(128)S(1)} %add_rsqrt_fusion.2) | copy-start | bytes 1540
  205.4 2.8 copy-start.2
  208.5 13.6 %copy-start.9 = (f32[128]{0:T(128)}, f32[128]{0:T(128)S(1)}, u32[]{:S(2)}) copy-start(f32[128]{0:T(128)S(1)} %add_rsqrt_fusion) | copy-start | bytes 1540
  222.1 47.4 %slice-start = ((f32[8,1,1024]{2,1,0:T(1,128)}), f32[1,1,1024]{2,1,0:T(1,128)S(1)}, s32[]{:S(2)}) async-start(f32[8,1,1024]{2,1,0:T(1,128)} %copy-done.2), calls=%async_computation.6 | async-start | bytes 8192 | tf_op jit(solution)/shard_map/slice | solution.py:13
  285.1 32.7 %copy-start.10 = (f32[128]{0:T(128)S(1)}, f32[128]{0:T(128)}, u32[]{:S(2)}) copy-start(f32[128]{0:T(128)} %copy-done.9) | copy-start | bytes 1540
  288.3 31.8 %copy-start.12 = (f32[128]{0:T(128)S(1)}, f32[128]{0:T(128)}, u32[]{:S(2)}) copy-start(f32[128]{0:T(128)} %copy-done.11) | copy-start | bytes 1540
  288.3 31.8 %copy-start.14 = (f32[128]{0:T(128)S(1)}, f32[128]{0:T(128)}, u32[]{:S(2)}) copy-start(f32[128]{0:T(128)} %copy-done.13) | copy-start | bytes 1540
  288.3 32.1 %copy-start.21 = (f32[128,512]{1,0:T(8,128)S(1)}, f32[128,512]{1,0:T(8,128)}, u32[]{:S(2)}) copy-start(f32[128,512]{1,0:T(8,128)} %get-tuple-element.480) | copy-start | bytes 786436
  290.4 60.3 %reduce-scatter.12.cloned.1.call-start = ((), (), s32[]{:S(2)}) async-start(), calls=%async_computation.5 | async-start | bytes 442368 | tf_op jit(solution)/shard_map/reduce_scatter | solution.py:212
Sparse Core Ops, SparseCore 0:
  25.5 28.6 reduce-scatter.9
  290.5 27.2 reduce-scatter.7
  321.7 28.8 reduce-scatter.11
